TPU v7x, 512 devices: a whole 4x4x16 slice. The times are simulated.
512 devices in a mesh: seq: 128 (over y, z, core), head: 4 (over x).
Axes of the slice: x: 4, y: 4, z: 16, core: 2. Of those that a mesh axis runs over, the one named last changes fastest.
Arguments:
- tokens: bfloat16 [64, 4, 1024], P('head'), may hold values from -6 to 6
- cache_keys: bfloat16 [64, 4096, 512], P(None, 'seq', 'head'), may hold values from -70 to 70
- cache_values: bfloat16 [64, 4096, 512], P(None, 'seq', 'head'), may hold values from -6 to 6
- held_states: bfloat16 [64, 512, 1024], P(None, 'seq'), may hold values from -6 to 6
- recompute_pos: int32 [64, 512], P(None, 'seq'), may hold values from 0 to 4095, as said below
- cache_len: int32 [64], replicated, may hold values from 1 to 4096
- new_prompt: int32 [64], replicated, may hold values 0 or 1
- w_qkv: bfloat16 [3, 1024, 512], P(None, None, 'head'), may hold values from -0.1875 to 0.1875
- qkv_bias: float32 [3, 512], P(None, 'head'), may hold values from -3 to 3
- w_out: bfloat16 [512, 1024], P('head'), may hold values from -1.5 to 1.5
- out_bias: float32 [1024], replicated, may hold values from -3 to 3
- attn_gain: float32 [1024], replicated, may hold values from 0.1 to 1.9
- attn_shift: float32 [1024], replicated, may hold values from -3 to 3
- w_up: bfloat16 [1024, 2048], P(None, 'head'), may hold values from -0.1875 to 0.1875
- up_bias: float32 [2048], P('head'), may hold values from -3 to 3
- w_down: bfloat16 [2048, 1024], P('head'), may hold values from -0.125 to 0.125
- down_bias: float32 [1024], replicated, may hold values from -3 to 3
- ffn_gain: float32 [1024], replicated, may hold values from 0.1 to 1.9
- ffn_shift: float32 [1024], replicated, may hold values from -3 to 3
Outputs:
- layer_out: bfloat16 [64, 4, 1024], P('head')
Inputs may be any that keep to these rules, and one draw needn't show every extreme that they name: `recompute_pos`: columns s * 4 to (s + 1) * 4 - 1 of a row hold distinct positions from s * 32 to (s + 1) * 32 - 1.
All inputs are finite; a program needn't handle non-finite values.
Results may differ from a plain program's by a relative error of at most 0.011.
Values may be sent and summed in bfloat16 or wider, within the bound.
No kernel may reach another device: no remote copies, remote signals or barrier semaphores. Data moves between devices by JAX's collectives and lax.ppermute only.
A program may use at most 192 MiB of HBM per device.

v0:
```python
import jax
import jax.numpy as jnp
from jax import lax
from jax.sharding import PartitionSpec as P

HDIM = 64
NEG = -1e30
EPS = 1e-05


def layer_norm(values, norm_gain, norm_bias):
    center = jnp.mean(values, axis=-1, keepdims=True)
    spread = values - center
    second = jnp.mean(spread * spread, axis=-1, keepdims=True)
    return spread * lax.rsqrt(second + EPS) * norm_gain + norm_bias


def merge_pair(first_part, second_part):
    first_max, first_sum, first_out = first_part
    second_max, second_sum, second_out = second_part
    joint_max = jnp.maximum(first_max, second_max)
    first_scale = jnp.exp(first_max - joint_max)
    second_scale = jnp.exp(second_max - joint_max)
    return (
        joint_max,
        first_sum * first_scale + second_sum * second_scale,
        first_out * first_scale[..., None] + second_out * second_scale[..., None],
    )


def partial_attention(queries, keys_here, values_here, visible):
    scores = jnp.einsum(
        "rthe,rphe->rthp", queries, keys_here, preferred_element_type=jnp.float32
    ) * HDIM ** (-0.5)
    highest = jnp.max(jnp.where(visible, scores, NEG), axis=-1)
    weights = jnp.exp(jnp.where(visible, scores - highest[..., None], NEG)).astype(jnp.bfloat16)
    totals = jnp.sum(weights.astype(jnp.float32), axis=-1)
    blended = jnp.einsum(
        "rthp,rphe->rthe", weights, values_here, preferred_element_type=jnp.float32
    )
    return (highest, totals, blended)


def on_device(
    tokens,
    cache_keys,
    cache_values,
    held_states,
    recompute_pos,
    cache_len,
    new_prompt,
    w_qkv,
    qkv_bias,
    w_out,
    out_bias,
    attn_gain,
    attn_shift,
    w_up,
    up_bias,
    w_down,
    down_bias,
    ffn_gain,
    ffn_shift,
):
    local_width = w_qkv.shape[2]
    local_heads = local_width // HDIM
    requests = cache_keys.shape[0]
    block_len = cache_keys.shape[1]
    own_rows = tokens.shape[0]
    steps_count = tokens.shape[1]
    block_rows = lax.all_gather(tokens, "head", axis=0, tiled=True)
    triple = (
        jnp.einsum("rtd,kdc->rtkc", block_rows, w_qkv, preferred_element_type=jnp.float32)
        + qkv_bias
    )
    triple = triple.astype(jnp.bfloat16).reshape(
        block_rows.shape[0], block_rows.shape[1], 3 * local_width
    )
    gathered = jnp.concatenate([triple, block_rows], axis=2)
    head_shape = (requests, steps_count, local_heads, HDIM)
    queries = gathered[:, :, :local_width].reshape(head_shape)
    new_keys = gathered[:, :, local_width : 2 * local_width].reshape(head_shape)
    new_values = gathered[:, :, 2 * local_width : 3 * local_width].reshape(head_shape)
    fresh_keys = (
        jnp.einsum("rjd,dc->rjc", held_states, w_qkv[1], preferred_element_type=jnp.float32)
        + qkv_bias[1]
    ).astype(jnp.bfloat16)
    offset_pos = lax.axis_index("seq") * block_len
    positions = jnp.arange(block_len, dtype=jnp.int32)
    matches = (recompute_pos - offset_pos)[:, :, None] == positions[None, None, :]
    placed = jnp.einsum(
        "rjp,rjc->rpc", matches.astype(jnp.bfloat16), fresh_keys, preferred_element_type=jnp.float32
    ).astype(jnp.bfloat16)
    replaced = jnp.any(matches, axis=1)
    keys_here = jnp.where(replaced[:, :, None], placed, cache_keys).reshape(
        requests, block_len, local_heads, HDIM
    )
    values_here = cache_values.reshape(requests, block_len, local_heads, HDIM)
    visible = ((offset_pos + positions)[None, :] < cache_len[:, None]) & (new_prompt[:, None] == 0)
    block_max, block_sum, block_out = partial_attention(
        queries, keys_here, values_here, visible[:, None, None, :]
    )
    cache_max = lax.pmax(block_max, "seq")
    factor = jnp.exp(block_max - cache_max)
    cache_sum, cache_out = lax.psum((block_sum * factor, block_out * factor[..., None]), "seq")
    order_t = jnp.arange(steps_count, dtype=jnp.int32)
    causal = (order_t[:, None] >= order_t[None, :])[None, :, None, :]
    new_max, new_sum, new_out = partial_attention(queries, new_keys, new_values, causal)
    joint_max, joint_sum, joint_out = merge_pair(
        (cache_max, cache_sum, cache_out), (new_max, new_sum, new_out)
    )
    attended = (
        (joint_out / joint_sum[..., None])
        .astype(jnp.bfloat16)
        .reshape(requests, steps_count, local_width)
    )
    head_terms = jnp.einsum("rtc,cd->rtd", attended, w_out, preferred_element_type=jnp.float32)
    summed = lax.psum(head_terms, "head")
    inputs_all = gathered[:, :, 3 * local_width :]
    normed_all = layer_norm(
        inputs_all.astype(jnp.float32) + summed + out_bias, attn_gain, attn_shift
    ).astype(jnp.bfloat16)
    hidden_all = jax.nn.gelu(
        jnp.einsum("rtd,df->rtf", normed_all, w_up, preferred_element_type=jnp.float32) + up_bias,
        approximate=False,
    ).astype(jnp.bfloat16)
    normed = lax.dynamic_slice_in_dim(normed_all, lax.axis_index("head") * own_rows, own_rows, 0)
    reduced = lax.psum_scatter(
        jnp.einsum("rtf,fd->rtd", hidden_all, w_down, preferred_element_type=jnp.float32),
        "head",
        scatter_dimension=0,
        tiled=True,
    )
    return layer_norm(normed.astype(jnp.float32) + reduced + down_bias, ffn_gain, ffn_shift).astype(
        jnp.bfloat16
    )


def solution(mesh):
    placed = (
        P("head", None, None),
        P(None, "seq", "head"),
        P(None, "seq", "head"),
        P(None, "seq", None),
        P(None, "seq"),
        P(),
        P(),
        P(None, None, "head"),
        P(None, "head"),
        P("head", None),
        P(),
        P(),
        P(),
        P(None, "head"),
        P("head"),
        P("head", None),
        P(),
        P(),
        P(),
    )
    return jax.shard_map(
        on_device, mesh=mesh, in_specs=placed, out_specs=P("head", None, None), check_vma=False
    )
```

profile of v0, /device:TPU:8, one launch (start us, length us, event | category | flops | bytes accessed | tf_op | source)
XLA Modules:
  0.0 722.2 jit_solution(1206370637751851345)
XLA Ops:
  6.5 0.8 copy-done.17
  8.1 1.5 fusion.9
  9.6 0.9 fusion
  11.5 13.3 %all_gather.3 = bf16[64,4,1024]{2,0,1:T(8,128)(2,1)S(1)} all-gather(bf16[16,4,1024]{2,0,1:T(8,128)(2,1)S(1)} %copy.59), channel_id=1, replica_groups=mesh['seq'=128,'head'=4] {'head'}, dimensions={0}, use_global_device_ids=true | all-gather | bytes 655360 | tf_op jit(solution)/shard_map/all_gather | solution.py:71
  25.2 0.7 fusion.119
  26.6 0.6 copy-done.18
  27.3 0.8 select_reduce_fusion
  28.7 215.2 %pmax.7 = f32[64,4,2]{0,1,2:T(4,128)S(1)} all-reduce(f32[64,4,2]{0,1,2:T(4,128)S(1)} %copy.68), channel_id=1, replica_groups=mesh['seq'=128,'head'=4] {'seq'}, use_global_device_ids=true, to_apply=%region_2.3 | all-reduce | flops 512 | bytes 4096 | tf_op jit(solution)/shard_map/pmax | solution.py:103
  244.0 0.7 copy.69
  245.1 2.0 fusion.5
  247.2 217.3 %psum.22 = f32[64,4,2]{0,1,2:T(4,128)S(1)} all-reduce(f32[64,4,2]{0,1,2:T(4,128)S(1)} %bitcast.79), channel_id=1, replica_groups=mesh['seq'=128,'head'=4] {'seq'}, use_global_device_ids=true, to_apply=%region_6.7 | all-reduce | flops 512 | bytes 4096 | tf_op jit(solution)/shard_map/psum | solution.py:105
  466.0 144.9 %all-reduce.3.cloned.1.call-done = f32[64,4,2,64]{3,1,2,0:T(4,128)} async-done(((f32[64,4,2,64]{3,1,2,0:T(4,128)}), f32[64,4,2,64]{3,1,2,0:T(4,128)}) %all-reduce.3.cloned.1.call-update) | async-done | bytes 131088 | tf_op jit(solution)/shard_map/psum | solution.py:105
  610.9 1.4 fusion.7
  612.6 0.7 copy-done.6
  613.3 1.3 fusion.30
  614.7 58.5 %all-reduce.5.cloned.1.call-done = f32[64,4,1024]{2,0,1:T(8,128)} async-done(((f32[64,4,1024]{2,0,1:T(8,128)}), f32[64,4,1024]{2,0,1:T(8,128)}) %all-reduce.5.cloned.1.call-update) | async-done | bytes 1048592 | tf_op jit(solution)/shard_map/psum | solution.py:118
  673.2 1.5 fusion.27
  676.1 0.9 copy-done.19
  677.0 0.6 fusion.69
  677.6 2.5 fusion.10
  680.1 32.6 %reduce-scatter.2.cloned.1.call-done = f32[16,4,1024]{2,0,1:T(8,128)} async-done(((f32[64,4,1024]{2,0,1:T(8,128)}), f32[16,4,1024]{2,0,1:T(8,128)}) %reduce-scatter.2.cloned.1.call-update) | async-done | bytes 262160 | tf_op jit(solution)/shard_map/reduce_scatter | solution.py:128
  712.7 1.1 fusion.76
  714.1 0.7 copy-done.14
  714.9 0.8 copy.83
  (86 shorter events, 7.3 us)
Async XLA Ops:
  6.5 671.0 %copy-start = (bf16[512,1024]{1,0:T(8,128)(2,1)S(1)}, bf16[512,1024]{1,0:T(8,128)(2,1)}, u32[]{:S(2)}) copy-start(bf16[512,1024]{1,0:T(8,128)(2,1)} %param.34) | copy-start | bytes 3145732
  6.5 604.4 %all-reduce.3.cloned.1.call-start = ((), (), s32[]{:S(2)}) async-start(), calls=%async_computation.1 | async-start | bytes 524288 | tf_op jit(solution)/shard_map/psum | solution.py:105
  6.5 0.8 copy-start.17
  7.4 0.7 copy-start.16
  8.1 1.5 copy-start.20
  10.5 0.9 copy-start.9
  11.4 13.3 %copy-start.3 = (bf16[3,1024,128]{2,1,0:T(8,128)(2,1)S(1)}, bf16[3,1024,128]{2,1,0:T(8,128)(2,1)}, u32[]{:S(2)}) copy-start(bf16[3,1024,128]{2,1,0:T(8,128)(2,1)} %param.26) | copy-start | bytes 2359300
  26.6 0.7 copy-start.7
  28.1 216.6 %copy-start.4 = (bf16[64,32,128]{2,1,0:T(8,128)(2,1)S(1)}, bf16[64,32,128]{2,1,0:T(8,128)(2,1)}, u32[]{:S(2)}) copy-start(bf16[64,32,128]{2,1,0:T(8,128)(2,1)} %param.21) | copy-start | bytes 1572868
  247.1 217.4 %copy-start.5 = (bf16[64,4,128]{2,0,1:T(8,128)(2,1)S(1)}, bf16[64,4,128]{2,0,1:T(8,128)(2,1)}, u32[]{:S(2)}) copy-start(bf16[64,4,128]{2,0,1:T(8,128)(2,1)} %get-tuple-element.15) | copy-start | bytes 196612
  247.1 217.5 %copy-start.8 = (bf16[64,4,2,64]{3,2,0,1:T(2,128)(2,1)S(1)}, bf16[64,4,2,64]{3,2,0,1:T(2,128)(2,1)}, u32[]{:S(2)}) copy-start(bf16[64,4,2,64]{3,2,0,1:T(2,128)(2,1)} %copy-done.7) | copy-start | bytes 196612
  247.1 426.1 %all-reduce.5.cloned.1.call-start = ((), (), s32[]{:S(2)}) async-start(), calls=%async_computation.2 | async-start | bytes 2097152 | tf_op jit(solution)/shard_map/psum | solution.py:118
  612.4 1.0 copy-start.6
  614.6 58.6 %copy-start.10 = (f32[1024]{0:T(1024)S(1)}, f32[1024]{0:T(1024)}, u32[]{:S(2)}) copy-start(f32[1024]{0:T(1024)} %param.29) | copy-start | bytes 12292
  614.7 98.1 %reduce-scatter.2.cloned.1.call-start = ((), (), s32[]{:S(2)}) async-start(), calls=%async_computation.3 | async-start | bytes 1310720 | tf_op jit(solution)/shard_map/reduce_scatter | solution.py:128
  673.2 1.5 copy-start.1
  674.8 0.7 copy-start.13
  675.1 0.7 copy-start.12
  675.8 1.2 copy-start.19
  675.8 1.2 copy-start.21
  680.1 32.6 %copy-start.11 = (f32[1024]{0:T(1024)S(1)}, f32[1024]{0:T(1024)}, u32[]{:S(2)}) copy-start(f32[1024]{0:T(1024)} %param.35) | copy-start | bytes 12292
  712.7 1.1 copy-start.2
  712.7 1.4 copy-start.15
  714.1 0.7 copy-start.14
  (2 other events, 1.3 us)
Sparse Core Ops, SparseCore 0:
  247.3 363.6 all-reduce.2
  614.8 58.4 all-reduce.4
  680.2 32.4 reduce-scatter.1
where the time goes:
time: 723 us; the launch traced here: 722 us
  blocking collectives  446 us (62%)
  waiting for transfers between devices  236 us (33%)
  between operations  13.4 us (2%)
  matrix products  11.8 us (2%)
  local copies, waits for them, and re-layouts  10.5 us (1%)
    psum x1, blocking collectives, on_device(): lax.psum((block_sum * factor, block_out * factor[..., None]), 'seq')  217 us
    pmax x1, blocking collectives, on_device(): cache_max = lax.pmax(block_max, 'seq')  215 us
    psum x1, waiting for transfers between devices, on_device(): lax.psum((block_sum * factor, block_out * factor[..., None]), 'seq')  145 us
    psum x1, waiting for transfers between devices, on_device(): summed = lax.psum(head_terms, 'head')  58.5 us
    reduce_scatter x1, waiting for transfers between devices, on_device(): lax.psum_scatter(jnp.einsum('rtf,fd->rtd', hidden_all, w_down, preferred_...  32.6 us
  transfers between devices with their start and end apart: 3, of which 3 were waited for; matrix products, arithmetic and copies ran while one was open for 0% of the time, Pallas kernels for 0%

commit v1 on v0

--- a/solution.py
+++ b/solution.py
@@ -115,7 +115,9 @@
         .reshape(requests, steps_count, local_width)
     )
     head_terms = jnp.einsum("rtc,cd->rtd", attended, w_out, preferred_element_type=jnp.float32)
-    summed = lax.psum(head_terms, "head")
+    summed = head_terms
+    for hop in (1, 2):
+        summed = summed + lax.ppermute(summed, "head", [(dev, dev ^ hop) for dev in range(4)])
     inputs_all = gathered[:, :, 3 * local_width :]
     normed_all = layer_norm(
         inputs_all.astype(jnp.float32) + summed + out_bias, attn_gain, attn_shift

time: 723 us -> 710 us (0.982)
  waiting for transfers between devices: 236 us -> 218 us
  starting transfers between devices: 0.09 us -> 8.31 us
    psum x1 -> x0, waiting for transfers between devices: 58.5 us -> none  [on_device(): summed = lax.psum(head_terms, 'head')]
    ppermute x0 -> x2, waiting for transfers between devices: none -> 43.9 us  [on_device(): lax.ppermute(summed, 'head', [(dev, dev ^ hop) for dev in range(4)])]
    ppermute x0 -> x2, starting transfers between devices: none -> 8.27 us  [on_device(): lax.ppermute(summed, 'head', [(dev, dev ^ hop) for dev in range(4)])]
  transfers between devices with their start and end apart: 3 -> 4, of which waited for: 3 -> 4; matrix products, arithmetic and copies ran while one was open for 0% -> 0% of each run, Pallas kernels for 0% -> 0%
where the time goes in v1:
time: 710 us
  blocking collectives  446 us (63%)
  waiting for transfers between devices  218 us (31%)
  between operations  13.8 us (2%)
  matrix products  10.8 us (2%)
  local copies, waits for them, and re-layouts  10 us (1%)
  starting transfers between devices  8.31 us (1%)
    psum x1, blocking collectives, on_device(): lax.psum((block_sum * factor, block_out * factor[..., None]), 'seq')  217 us
    pmax x1, blocking collectives, on_device(): cache_max = lax.pmax(block_max, 'seq')  215 us
    psum x1, waiting for transfers between devices, on_device(): lax.psum((block_sum * factor, block_out * factor[..., None]), 'seq')  145 us
    ppermute x2, waiting for transfers between devices, on_device(): lax.ppermute(summed, 'head', [(dev, dev ^ hop) for dev in range(4)])  43.9 us
    reduce_scatter x1, waiting for transfers between devices, on_device(): lax.psum_scatter(jnp.einsum('rtf,fd->rtd', hidden_all, w_down, preferred_...  28.9 us
  transfers between devices with their start and end apart: 4, of which 4 were waited for; matrix products, arithmetic and copies ran while one was open for 0% of the time, Pallas kernels for 0%

profile of v1, /device:TPU:8, one launch (start us, length us, event | category | flops | bytes accessed | tf_op | source)
XLA Modules:
  0.0 709.7 jit_solution(1287097058378115641)
XLA Ops:
  6.5 0.8 copy-done.16
  8.1 1.5 fusion.9
  9.6 0.9 fusion
  11.5 13.3 %all_gather.3 = bf16[64,4,1024]{2,0,1:T(8,128)(2,1)S(1)} all-gather(bf16[16,4,1024]{2,0,1:T(8,128)(2,1)S(1)} %copy.59), channel_id=1, replica_groups=mesh['seq'=128,'head'=4] {'head'}, dimensions={0}, use_global_device_ids=true | all-gather | bytes 655360 | tf_op jit(solution)/shard_map/all_gather | solution.py:71
  25.2 0.7 fusion.119
  26.6 0.6 copy-done.17
  27.3 0.8 select_reduce_fusion
  28.7 215.2 %pmax.7 = f32[64,4,2]{0,1,2:T(4,128)S(1)} all-reduce(f32[64,4,2]{0,1,2:T(4,128)S(1)} %copy.68), channel_id=1, replica_groups=mesh['seq'=128,'head'=4] {'seq'}, use_global_device_ids=true, to_apply=%region_2.3 | all-reduce | flops 512 | bytes 4096 | tf_op jit(solution)/shard_map/pmax | solution.py:103
  244.0 0.7 copy.69
  245.1 2.0 fusion.5
  247.2 217.3 %psum.15 = f32[64,4,2]{0,1,2:T(4,128)S(1)} all-reduce(f32[64,4,2]{0,1,2:T(4,128)S(1)} %bitcast.79), channel_id=1, replica_groups=mesh['seq'=128,'head'=4] {'seq'}, use_global_device_ids=true, to_apply=%region_6.7 | all-reduce | flops 512 | bytes 4096 | tf_op jit(solution)/shard_map/psum | solution.py:105
  466.0 144.9 %all-reduce.2.cloned.1.call-done = f32[64,4,2,64]{3,1,2,0:T(4,128)} async-done(((f32[64,4,2,64]{3,1,2,0:T(4,128)}), f32[64,4,2,64]{3,1,2,0:T(4,128)}) %all-reduce.2.cloned.1.call-update) | async-done | bytes 131088 | tf_op jit(solution)/shard_map/psum | solution.py:105
  610.9 1.4 fusion.7
  612.6 0.7 copy-done.5
  613.6 3.4 collective-permute-start
  617.0 22.4 %collective-permute-done = f32[64,4,1024]{2,0,1:T(8,128)S(1)} collective-permute-done((f32[64,4,1024]{2,0,1:T(8,128)S(1)}, f32[64,4,1024]{2,0,1:T(8,128)S(1)}, u32[]{:S(2)}, u32[]{:S(2)}) %collective-permute-start) | collective-permute-done | bytes 1048608 | tf_op jit(solution)/shard_map/ppermute | solution.py:120
  639.5 4.9 collective-permute-start.1
  644.4 21.5 %collective-permute-done.1 = f32[64,4,1024]{2,0,1:T(8,128)S(1)} collective-permute-done((f32[64,4,1024]{2,0,1:T(8,128)S(1)}, f32[64,4,1024]{2,0,1:T(8,128)S(1)}, u32[]{:S(2)}, u32[]{:S(2)}) %collective-permute-start.1) | collective-permute-done | bytes 1048608 | tf_op jit(solution)/shard_map/ppermute | solution.py:120
  667.9 0.6 fusion.68
  668.5 2.5 fusion.10
  671.0 28.9 %reduce-scatter.2.cloned.1.call-done = f32[16,4,1024]{2,0,1:T(8,128)} async-done(((f32[64,4,1024]{2,0,1:T(8,128)}), f32[16,4,1024]{2,0,1:T(8,128)}) %reduce-scatter.2.cloned.1.call-update) | async-done | bytes 262160 | tf_op jit(solution)/shard_map/reduce_scatter | solution.py:130
  700.0 1.1 fusion.75
  701.4 0.7 copy-done.12
  702.1 0.8 copy.83
  (86 shorter events, 8.4 us)
Async XLA Ops:
  6.5 662.0 %copy-start = (bf16[512,1024]{1,0:T(8,128)(2,1)S(1)}, bf16[512,1024]{1,0:T(8,128)(2,1)}, u32[]{:S(2)}) copy-start(bf16[512,1024]{1,0:T(8,128)(2,1)} %param.34) | copy-start | bytes 3145732
  6.5 604.4 %all-reduce.2.cloned.1.call-start = ((), (), s32[]{:S(2)}) async-start(), calls=%async_computation.1 | async-start | bytes 524288 | tf_op jit(solution)/shard_map/psum | solution.py:105
  6.5 0.8 copy-start.16
  7.4 0.7 copy-start.15
  8.1 1.5 copy-start.19
  10.5 0.9 copy-start.8
  11.4 13.3 %copy-start.2 = (bf16[3,1024,128]{2,1,0:T(8,128)(2,1)S(1)}, bf16[3,1024,128]{2,1,0:T(8,128)(2,1)}, u32[]{:S(2)}) copy-start(bf16[3,1024,128]{2,1,0:T(8,128)(2,1)} %param.26) | copy-start | bytes 2359300
  26.6 0.7 copy-start.6
  28.1 216.6 %copy-start.3 = (bf16[64,32,128]{2,1,0:T(8,128)(2,1)S(1)}, bf16[64,32,128]{2,1,0:T(8,128)(2,1)}, u32[]{:S(2)}) copy-start(bf16[64,32,128]{2,1,0:T(8,128)(2,1)} %param.21) | copy-start | bytes 1572868
  247.1 217.4 %copy-start.4 = (bf16[64,4,128]{2,0,1:T(8,128)(2,1)S(1)}, bf16[64,4,128]{2,0,1:T(8,128)(2,1)}, u32[]{:S(2)}) copy-start(bf16[64,4,128]{2,0,1:T(8,128)(2,1)} %get-tuple-element.17) | copy-start | bytes 196612
  247.1 217.5 %copy-start.7 = (bf16[64,4,2,64]{3,2,0,1:T(2,128)(2,1)S(1)}, bf16[64,4,2,64]{3,2,0,1:T(2,128)(2,1)}, u32[]{:S(2)}) copy-start(bf16[64,4,2,64]{3,2,0,1:T(2,128)(2,1)} %copy-done.6) | copy-start | bytes 196612
  247.1 452.8 %reduce-scatter.2.cloned.1.call-start = ((), (), s32[]{:S(2)}) async-start(), calls=%async_computation.2 | async-start | bytes 1310720 | tf_op jit(solution)/shard_map/reduce_scatter | solution.py:130
  612.4 1.0 copy-start.5
  613.6 52.3 %copy-start.14 = (f32[1024]{0:T(1024)S(1)}, f32[1024]{0:T(1024)}, u32[]{:S(2)}) copy-start(f32[1024]{0:T(1024)} %param.29) | copy-start | bytes 12292
  613.6 25.8 %collective-permute-start = (f32[64,4,1024]{2,0,1:T(8,128)S(1)}, f32[64,4,1024]{2,0,1:T(8,128)S(1)}, u32[]{:S(2)}, u32[]{:S(2)}) collective-permute-start(f32[64,4,1024]{2,0,1:T(8,128)S(1)} %fusion.29), channel_id=1, source_target_pairs={{0,1},{1,0},{2,3},{3,2},{4,5},{5,4},{6,7},{7,6},{8,9},{9,8},{10,11... | collective-permute-start | bytes 3145736 | tf_op jit(solution)/shard_map/ppermute | solution.py:120
  639.5 26.4 %collective-permute-start.1 = (f32[64,4,1024]{2,0,1:T(8,128)S(1)}, f32[64,4,1024]{2,0,1:T(8,128)S(1)}, u32[]{:S(2)}, u32[]{:S(2)}) collective-permute-start(f32[64,4,1024]{2,0,1:T(8,128)S(1)} %add.126), channel_id=1, source_target_pairs={{0,2},{1,3},{2,0},{3,1},{4,6},{5,7},{6,4},{7,5},{8,10},{9,11},{10,... | collective-permute-start | bytes 3145736 | tf_op jit(solution)/shard_map/ppermute | solution.py:120
  666.2 0.7 copy-start.11
  666.5 0.7 copy-start.10
  666.5 1.2 copy-start.18
  667.1 0.8 copy-start.20
  671.0 29.0 %copy-start.9 = (f32[1024]{0:T(1024)S(1)}, f32[1024]{0:T(1024)}, u32[]{:S(2)}) copy-start(f32[1024]{0:T(1024)} %param.35) | copy-start | bytes 12292
  700.0 1.1 copy-start.1
  700.0 1.4 copy-start.13
  701.3 0.7 copy-start.12
  (2 other events, 1.3 us)
Sparse Core Ops, SparseCore 0:
  247.3 363.6 all-reduce.1
  671.2 28.7 reduce-scatter.1
